TPU v7x, 128 devices: a whole 4x4x4 slice. The times are simulated.
128 devices in a mesh: row: 16 (over z, y), col: 8 (over x, core).
Axes of the slice: x: 4, y: 4, z: 4, core: 2. Of those that a mesh axis runs over, the one named last changes fastest.
Arguments:
- queries: float32 [32768, 256], P(('row', 'col')), may hold values from -1 to 1
- passages: float32 [32768, 256], P(('col', 'row')), may hold values from -1 to 1
- mean_cost: float32 [1], replicated, may hold values from 1 to 3
Outputs:
- row_potential: float32 [32768], P('row')
- col_potential: float32 [32768], P('col')
All inputs are finite; a program needn't handle non-finite values.
Results may differ from a plain program's by a relative error of at most 0.0003.
Values sent between devices are 32-bit elements; how exact they have to be, the bound alone decides.
No kernel may reach another device: no remote copies, remote signals or barrier semaphores. Data moves between devices by JAX's collectives and lax.ppermute only.
A program may use at most 256 MiB of HBM per device.

v0:
```python
import math
import jax
import jax.numpy as jnp
from jax import lax
from jax.sharding import PartitionSpec as P

ITERS = 3


def inner_costs(left, right):
    left_norms = jnp.sum(left * left, axis=1)
    right_norms = jnp.sum(right * right, axis=1)
    inner = lax.dot_general(
        left,
        right,
        (((1,), (1,)), ((), ())),
        precision=lax.Precision.HIGHEST,
        preferred_element_type=jnp.float32,
    )
    return left_norms[:, None] + right_norms[None, :] - 2.0 * inner


def digit_partners(axis, size, stride, width, shift):
    perm = []
    for i in range(size):
        p = i // stride % width
        perm.append((i, i + ((p + shift) % width - p) * stride))
    return perm


def exchange(x, axis, stride, width):
    size = lax.axis_size(axis)
    pos = lax.axis_index(axis) // stride % width
    received = [x] + [
        lax.ppermute(x, axis, digit_partners(axis, size, stride, width, k)) for k in range(1, width)
    ]
    stacked = jnp.stack(received)
    return [
        lax.dynamic_index_in_dim(stacked, (pos - q) % width, 0, keepdims=False)
        for q in range(width)
    ]


def combine_over(peak, total, axis, digits):
    size = lax.axis_size(axis)
    packed = jnp.stack([peak, total])
    stride = 1
    for width in digits:
        parts = [packed] + [
            lax.ppermute(packed, axis, digit_partners(axis, size, stride, width, k))
            for k in range(1, width)
        ]
        new_peak = parts[0][0]
        for part in parts[1:]:
            new_peak = jnp.maximum(new_peak, part[0])
        terms = [part[1] * jnp.exp(part[0] - new_peak) for part in parts]
        if width == 4:
            new_total = terms[0] + terms[2] + (terms[1] + terms[3])
        else:
            new_total = terms[0] + terms[1]
        packed = jnp.stack([new_peak, new_total])
        stride *= width
    return packed[0] + jnp.log(packed[1])


def radix_digits(size):
    digits = []
    while size > 1:
        width = 4 if size % 4 == 0 else 2
        digits.append(width)
        size //= width
    return tuple(digits)


def col_digits(size):
    if size % 2 == 0:
        return (2,) + radix_digits(size // 2)
    return radix_digits(size)


def logsum_col(gaps, scale):
    peak = jnp.max(gaps, axis=1) / scale
    totals = jnp.sum(jnp.exp(gaps / scale - peak[:, None]), axis=1)
    return combine_over(peak, totals, "col", col_digits(lax.axis_size("col")))


def logsum_row(gaps, scale):
    peak = jnp.max(gaps, axis=0) / scale
    totals = jnp.sum(jnp.exp(gaps / scale - peak[None, :]), axis=0)
    return combine_over(peak, totals, "row", radix_digits(lax.axis_size("row")))


def gather_col(x):
    size = lax.axis_size("col")
    return jnp.concatenate(exchange(x, "col", 1, size), axis=0)


def gather_row(x):
    stride = 1
    for width in radix_digits(lax.axis_size("row")):
        x = jnp.concatenate(exchange(x, "row", stride, width), axis=0)
        stride *= width
    return x


def per_device(queries, passages, mean_cost):
    entropy_scale = 0.1 * mean_cost[0]
    row_count = lax.axis_size("row")
    col_count = lax.axis_size("col")
    all_queries = queries.shape[0] * row_count * col_count
    all_passages = passages.shape[0] * row_count * col_count
    query_block = gather_col(queries)
    rows = passages.shape[0]
    split = rows - rows * 5 // 32
    passage_block = jnp.concatenate(
        [lax.all_gather(passages[:split], "row", axis=0, tiled=True), gather_row(passages[split:])],
        axis=0,
    )
    cost_tile = inner_costs(query_block, passage_block)
    col_potential = jnp.zeros((cost_tile.shape[1],), jnp.float32)
    row_potential = jnp.zeros((cost_tile.shape[0],), jnp.float32)
    for repeat in range(ITERS):
        gaps = col_potential[None, :] - cost_tile
        row_potential = -entropy_scale * math.log(all_queries) - entropy_scale * logsum_col(
            gaps, entropy_scale
        )
        gaps = row_potential[:, None] - cost_tile
        col_potential = -entropy_scale * math.log(all_passages) - entropy_scale * logsum_row(
            gaps, entropy_scale
        )
    head = col_potential[: split * row_count].reshape(row_count, split)
    tail = col_potential[split * row_count :].reshape(row_count, rows - split)
    return (row_potential, jnp.concatenate([head, tail], axis=1).reshape(-1))


def solution(mesh):
    placed = (P(("row", "col"), None), P(("col", "row"), None), P())
    return jax.shard_map(
        per_device, mesh=mesh, in_specs=placed, out_specs=(P("row"), P("col")), check_vma=False
    )
```

profile of v0, /device:TPU:0, one launch (start us, length us, event | category | flops | bytes accessed | tf_op | source)
XLA Modules:
  0.0 269.4 jit_solution(6732371264932919641)
XLA Ops:
  11.4 2.9 %collective-permute-start.8 = (f32[40,256]{1,0:T(8,128)S(1)}, f32[40,256]{1,0:T(8,128)S(1)}, u32[]{:S(2)}, u32[]{:S(2)}) collective-permute-start(f32[40,256]{1,0:T(8,128)S(1)} %get-tuple-element.7), channel_id=1, source_target_pairs={{0,16},{8,24},{16,0},{24,8},{32,48},{40,56},{48,32},{56,40},{64,80... | collective-permute-start | bytes 122888 | tf_op jit(solution)/shard_map/ppermute | solution.py:35
  20.4 3.6 %collective-permute-start.11 = (f32[160,256]{1,0:T(8,128)S(1)}, f32[160,256]{1,0:T(8,128)S(1)}, u32[]{:S(2)}, u32[]{:S(2)}) collective-permute-start(f32[160,256]{1,0:T(8,128)S(1)} %get-tuple-element.9), channel_id=1, source_target_pairs={{0,64},{8,72},{16,80},{24,88},{32,96},{40,104},{48,112},{56,120},{... | collective-permute-start | bytes 491528 | tf_op jit(solution)/shard_map/ppermute | solution.py:35
  29.3 5.5 %collective-permute-done.11 = f32[160,256]{1,0:T(8,128)S(1)} collective-permute-done((f32[160,256]{1,0:T(8,128)S(1)}, f32[160,256]{1,0:T(8,128)S(1)}, u32[]{:S(2)}, u32[]{:S(2)}) %collective-permute-start.11) | collective-permute-done | bytes 163872 | tf_op jit(solution)/shard_map/ppermute | solution.py:35
  39.8 5.0 %collective-permute-done.3 = f32[256,256]{1,0:T(8,128)S(1)} collective-permute-done((f32[256,256]{1,0:T(8,128)}, f32[256,256]{1,0:T(8,128)S(1)}, u32[]{:S(2)}, u32[]{:S(2)}) %collective-permute-start.3) | collective-permute-done | bytes 262176 | tf_op jit(solution)/shard_map/ppermute | solution.py:35
  45.6 7.9 %collective-permute-done.5 = f32[256,256]{1,0:T(8,128)S(1)} collective-permute-done((f32[256,256]{1,0:T(8,128)S(1)}, f32[256,256]{1,0:T(8,128)S(1)}, u32[]{:S(2)}, u32[]{:S(2)}) %collective-permute-start.5) | collective-permute-done | bytes 262176 | tf_op jit(solution)/shard_map/ppermute | solution.py:35
  56.2 7.0 %all-gather.2.cloned.1.call-done = f32[3456,256]{1,0:T(8,128)} async-done(((f32[216,256]{1,0:T(8,128)}), f32[3456,256]{1,0:T(8,128)}) %all-gather.2.cloned.1.call-update) | async-done | bytes 3538960 | tf_op jit(solution)/shard_map/all_gather | solution.py:116
  66.2 34.8 %subtract_reduce_fusion.5 = (f32[2048]{0:T(1024)S(1)}, f32[2048,4096]{1,0:T(8,128)}) fusion(f32[2048,256]{1,0:T(8,128)S(1)} %bitcast_dynamic-update-slice_fusion, f32[4096,256]{1,0:T(8,128)S(1)} %bitcast_dynamic-update-slice_fusion.16, f32[4096]{0:T(1024)S(1)} %multiply_reduce_fusion, f32[2048]{0:T(1024)S(1)} %multiply_reduce_fusion.1), kind=kOutput, calls=%fused_computation.12 | convolution fusion | flops 25811744768 | bytes 39878656 | tf_op jit(solution)/shard_map/dot_general | solution.py:13
  101.0 14.5 %exponential_reduce_fusion.5 = f32[2048]{0:T(1024)S(1)} fusion(f32[2048,4096]{1,0:T(8,128)} %get-tuple-element.59, f32[2048]{0:T(1024)S(1)} %broadcast_divide_fusion.5, f32[]{:T(128)} %bitcast), kind=kLoop, calls=%fused_computation.5 | loop fusion | flops 33552384 | bytes 33570820 | tf_op jit(solution)/shard_map/reduce_sum | solution.py:83
  124.9 13.8 %subtract_reduce_fusion.4 = f32[4096]{0:T(1024)S(1)} fusion(f32[2048,4096]{1,0:T(8,128)} %get-tuple-element.59, f32[2048]{0:T(1024)S(1)} %multiply_subtract_fusion.6), kind=kLoop, calls=%fused_computation.11 | loop fusion | flops 16773120 | bytes 33579008 | tf_op jit(solution)/shard_map/reduce_max | solution.py:88
  138.7 6.3 %copy-done = f32[2048,4096]{1,0:T(8,128)S(1)} copy-done((f32[2048,4096]{1,0:T(8,128)S(1)}, f32[2048,4096]{1,0:T(8,128)}, u32[]{:S(2)}) %copy-start) | copy-done | bytes 33554456
  145.0 7.6 %exponential_reduce_fusion.4 = f32[4096]{0:T(1024)S(1)} fusion(f32[2048,4096]{1,0:T(8,128)S(1)} %copy-done, f32[4096]{0:T(1024)S(1)} %broadcast_divide_fusion.2, f32[2048]{0:T(1024)S(1)} %multiply_subtract_fusion.6, f32[]{:T(128)} %bitcast), kind=kLoop, calls=%fused_computation.4 | loop fusion | flops 33550336 | bytes 33595396 | tf_op jit(solution)/shard_map/reduce_sum | solution.py:89
  153.5 2.7 %collective-permute-start.18 = (f32[2,4096]{1,0:T(2,128)S(1)}, f32[2,4096]{1,0:T(2,128)S(1)}, u32[]{:S(2)}, u32[]{:S(2)}) collective-permute-start(f32[2,4096]{1,0:T(2,128)S(1)} %pad_maximum_fusion.3), channel_id=1, source_target_pairs={{0,16},{8,24},{16,0},{24,8},{32,48},{40,56},{48,32},{56,40},{64,80... | collective-permute-start | bytes 98312 | tf_op jit(solution)/shard_map/ppermute | solution.py:50
  167.2 3.0 %subtract_reduce_fusion.3 = f32[2048]{0:T(1024)S(1)} fusion(f32[2048,4096]{1,0:T(8,128)S(1)} %copy-done, f32[4096]{0:T(1024)S(1)} %bitcast.126), kind=kLoop, calls=%fused_computation.10 | loop fusion | flops 16775168 | bytes 33579008 | tf_op jit(solution)/shard_map/reduce_max | solution.py:82
  170.2 8.0 %exponential_reduce_fusion.3 = f32[2048]{0:T(1024)S(1)} fusion(f32[2048,4096]{1,0:T(8,128)S(1)} %copy-done, f32[2048]{0:T(1024)S(1)} %broadcast_divide_fusion.4, f32[4096]{0:T(1024)S(1)} %bitcast.127, f32[]{:T(128)} %bitcast), kind=kLoop, calls=%fused_computation.3 | loop fusion | flops 33552384 | bytes 33587204 | tf_op jit(solution)/shard_map/reduce_sum | solution.py:83
  180.0 3.8 %collective-permute-start.25 = (f32[2,2048]{1,0:T(2,128)S(1)}, f32[2,2048]{1,0:T(2,128)S(1)}, u32[]{:S(2)}, u32[]{:S(2)}) collective-permute-start(f32[2,2048]{1,0:T(2,128)S(1)} %pad_maximum_fusion.12), channel_id=1, source_target_pairs={{0,4},{1,5},{2,6},{3,7},{4,0},{5,1},{6,2},{7,3},{8,12},{9,13},{10,... | collective-permute-start | bytes 49160 | tf_op jit(solution)/shard_map/ppermute | solution.py:50
  187.6 4.7 %subtract_reduce_fusion.2 = f32[4096]{0:T(1024)S(1)} fusion(f32[2048,4096]{1,0:T(8,128)S(1)} %copy-done, f32[2048]{0:T(1024)S(1)} %multiply_subtract_fusion.5), kind=kLoop, calls=%fused_computation.9 | loop fusion | flops 16773120 | bytes 33579008 | tf_op jit(solution)/shard_map/reduce_max | solution.py:88
  192.3 7.6 %exponential_reduce_fusion.2 = f32[4096]{0:T(1024)S(1)} fusion(f32[2048,4096]{1,0:T(8,128)S(1)} %copy-done, f32[4096]{0:T(1024)S(1)} %broadcast_divide_fusion.1, f32[2048]{0:T(1024)S(1)} %multiply_subtract_fusion.5, f32[]{:T(128)} %bitcast), kind=kLoop, calls=%fused_computation.2 | loop fusion | flops 33550336 | bytes 33595396 | tf_op jit(solution)/shard_map/reduce_sum | solution.py:89
  201.5 2.7 %collective-permute-start.28 = (f32[2,4096]{1,0:T(2,128)S(1)}, f32[2,4096]{1,0:T(2,128)S(1)}, u32[]{:S(2)}, u32[]{:S(2)}) collective-permute-start(f32[2,4096]{1,0:T(2,128)S(1)} %pad_maximum_fusion.5), channel_id=1, source_target_pairs={{0,16},{8,24},{16,0},{24,8},{32,48},{40,56},{48,32},{56,40},{64,80... | collective-permute-start | bytes 98312 | tf_op jit(solution)/shard_map/ppermute | solution.py:50
  216.5 3.0 %subtract_reduce_fusion.1 = f32[2048]{0:T(1024)S(1)} fusion(f32[2048,4096]{1,0:T(8,128)S(1)} %copy-done, f32[4096]{0:T(1024)S(1)} %bitcast.128), kind=kLoop, calls=%fused_computation.8 | loop fusion | flops 16775168 | bytes 33579008 | tf_op jit(solution)/shard_map/reduce_max | solution.py:82
  219.5 8.0 %exponential_reduce_fusion.1 = f32[2048]{0:T(1024)S(1)} fusion(f32[2048,4096]{1,0:T(8,128)S(1)} %copy-done, f32[2048]{0:T(1024)S(1)} %broadcast_divide_fusion.3, f32[4096]{0:T(1024)S(1)} %bitcast.129, f32[]{:T(128)} %bitcast), kind=kLoop, calls=%fused_computation.1 | loop fusion | flops 33552384 | bytes 33587204 | tf_op jit(solution)/shard_map/reduce_sum | solution.py:83
  229.0 2.7 %collective-permute-start.35 = (f32[2,2048]{1,0:T(2,128)S(1)}, f32[2,2048]{1,0:T(2,128)S(1)}, u32[]{:S(2)}, u32[]{:S(2)}) collective-permute-start(f32[2,2048]{1,0:T(2,128)S(1)} %pad_maximum_fusion.14), channel_id=1, source_target_pairs={{0,4},{1,5},{2,6},{3,7},{4,0},{5,1},{6,2},{7,3},{8,12},{9,13},{10,... | collective-permute-start | bytes 49160 | tf_op jit(solution)/shard_map/ppermute | solution.py:50
  235.5 4.7 %subtract_reduce_fusion = f32[4096]{0:T(1024)S(1)} fusion(f32[2048,4096]{1,0:T(8,128)S(1)} %copy-done, f32[2048]{0:T(1024)S(1)} %multiply_subtract_fusion.4), kind=kLoop, calls=%fused_computation.7 | loop fusion | flops 16773120 | bytes 33579008 | tf_op jit(solution)/shard_map/reduce_max | solution.py:88
  240.2 7.6 %exponential_reduce_fusion = f32[4096]{0:T(1024)S(1)} fusion(f32[2048,4096]{1,0:T(8,128)S(1)} %copy-done, f32[4096]{0:T(1024)S(1)} %broadcast_divide_fusion, f32[2048]{0:T(1024)S(1)} %multiply_subtract_fusion.4, f32[]{:T(128)} %bitcast), kind=kLoop, calls=%fused_computation | loop fusion | flops 33550336 | bytes 33595396 | tf_op jit(solution)/shard_map/reduce_sum | solution.py:89
  254.9 2.7 %collective-permute-start.41 = (f32[2,4096]{1,0:T(2,128)S(1)}, f32[2,4096]{1,0:T(2,128)S(1)}, u32[]{:S(2)}, u32[]{:S(2)}) collective-permute-start(f32[2,4096]{1,0:T(2,128)S(1)} %pad_maximum_fusion.8), channel_id=1, source_target_pairs={{0,64},{8,72},{16,80},{24,88},{32,96},{40,104},{48,112},{56,120},{... | collective-permute-start | bytes 98312 | tf_op jit(solution)/shard_map/ppermute | solution.py:50
  (159 shorter events, 83.5 us)
Async XLA Ops:
  7.2 56.0 %all-gather.2.cloned.1.call-start = ((), (), s32[]{:S(2)}) async-start(), calls=%async_computation | async-start | bytes 3760128 | tf_op jit(solution)/shard_map/all_gather | solution.py:116
  9.7 8.1 %collective-permute-start.7 = (f32[40,256]{1,0:T(8,128)S(1)}, f32[40,256]{1,0:T(8,128)S(1)}, u32[]{:S(2)}, u32[]{:S(2)}) collective-permute-start(f32[40,256]{1,0:T(8,128)S(1)} %get-tuple-element.7), channel_id=1, source_target_pairs={{0,8},{8,16},{16,24},{24,0},{32,40},{40,48},{48,56},{56,32},{64,72... | collective-permute-start | bytes 122888 | tf_op jit(solution)/shard_map/ppermute | solution.py:35
  11.4 6.5 %collective-permute-start.8 = (f32[40,256]{1,0:T(8,128)S(1)}, f32[40,256]{1,0:T(8,128)S(1)}, u32[]{:S(2)}, u32[]{:S(2)}) collective-permute-start(f32[40,256]{1,0:T(8,128)S(1)} %get-tuple-element.7), channel_id=1, source_target_pairs={{0,16},{8,24},{16,0},{24,8},{32,48},{40,56},{48,32},{56,40},{64,80... | collective-permute-start | bytes 122888 | tf_op jit(solution)/shard_map/ppermute | solution.py:35
  15.6 22.1 %collective-permute-start = (f32[256,256]{1,0:T(8,128)}, f32[256,256]{1,0:T(8,128)S(1)}, u32[]{:S(2)}, u32[]{:S(2)}) collective-permute-start(f32[256,256]{1,0:T(8,128)} %param.3), channel_id=1, source_target_pairs={{0,1},{1,2},{2,3},{3,4},{4,5},{5,6},{6,7},{7,0},{8,9},{9,10},{10,1... | collective-permute-start | bytes 786440 | tf_op jit(solution)/shard_map/ppermute | solution.py:35
  15.6 23.4 %collective-permute-start.1 = (f32[256,256]{1,0:T(8,128)}, f32[256,256]{1,0:T(8,128)S(1)}, u32[]{:S(2)}, u32[]{:S(2)}) collective-permute-start(f32[256,256]{1,0:T(8,128)} %param.3), channel_id=1, source_target_pairs={{0,2},{1,3},{2,4},{3,5},{4,6},{5,7},{6,0},{7,1},{8,10},{9,11},{10,... | collective-permute-start | bytes 786440 | tf_op jit(solution)/shard_map/ppermute | solution.py:35
  18.4 9.4 %collective-permute-start.10 = (f32[160,256]{1,0:T(8,128)S(1)}, f32[160,256]{1,0:T(8,128)S(1)}, u32[]{:S(2)}, u32[]{:S(2)}) collective-permute-start(f32[160,256]{1,0:T(8,128)S(1)} %get-tuple-element.9), channel_id=1, source_target_pairs={{0,32},{8,40},{16,48},{24,56},{32,64},{40,72},{48,80},{56,88},{64,... | collective-permute-start | bytes 491528 | tf_op jit(solution)/shard_map/ppermute | solution.py:35
  20.4 14.5 %collective-permute-start.11 = (f32[160,256]{1,0:T(8,128)S(1)}, f32[160,256]{1,0:T(8,128)S(1)}, u32[]{:S(2)}, u32[]{:S(2)}) collective-permute-start(f32[160,256]{1,0:T(8,128)S(1)} %get-tuple-element.9), channel_id=1, source_target_pairs={{0,64},{8,72},{16,80},{24,88},{32,96},{40,104},{48,112},{56,120},{... | collective-permute-start | bytes 491528 | tf_op jit(solution)/shard_map/ppermute | solution.py:35
  23.9 12.1 %collective-permute-start.12 = (f32[160,256]{1,0:T(8,128)S(1)}, f32[160,256]{1,0:T(8,128)S(1)}, u32[]{:S(2)}, u32[]{:S(2)}) collective-permute-start(f32[160,256]{1,0:T(8,128)S(1)} %get-tuple-element.9), channel_id=1, source_target_pairs={{0,96},{8,104},{16,112},{24,120},{32,0},{40,8},{48,16},{56,24},{64... | collective-permute-start | bytes 491528 | tf_op jit(solution)/shard_map/ppermute | solution.py:35
  27.8 12.0 %collective-permute-start.2 = (f32[256,256]{1,0:T(8,128)}, f32[256,256]{1,0:T(8,128)S(1)}, u32[]{:S(2)}, u32[]{:S(2)}) collective-permute-start(f32[256,256]{1,0:T(8,128)} %param.3), channel_id=1, source_target_pairs={{0,3},{1,4},{2,5},{3,6},{4,7},{5,0},{6,1},{7,2},{8,11},{9,12},{10,... | collective-permute-start | bytes 786440 | tf_op jit(solution)/shard_map/ppermute | solution.py:35
  34.8 10.0 %collective-permute-start.3 = (f32[256,256]{1,0:T(8,128)}, f32[256,256]{1,0:T(8,128)S(1)}, u32[]{:S(2)}, u32[]{:S(2)}) collective-permute-start(f32[256,256]{1,0:T(8,128)} %param.3), channel_id=1, source_target_pairs={{0,4},{1,5},{2,6},{3,7},{4,0},{5,1},{6,2},{7,3},{8,12},{9,13},{10,... | collective-permute-start | bytes 786440 | tf_op jit(solution)/shard_map/ppermute | solution.py:35
  36.1 9.5 %collective-permute-start.4 = (f32[256,256]{1,0:T(8,128)}, f32[256,256]{1,0:T(8,128)S(1)}, u32[]{:S(2)}, u32[]{:S(2)}) collective-permute-start(f32[256,256]{1,0:T(8,128)} %param.3), channel_id=1, source_target_pairs={{0,5},{1,6},{2,7},{3,0},{4,1},{5,2},{6,3},{7,4},{8,13},{9,14},{10,... | collective-permute-start | bytes 786440 | tf_op jit(solution)/shard_map/ppermute | solution.py:35
  37.8 15.7 %collective-permute-start.5 = (f32[256,256]{1,0:T(8,128)S(1)}, f32[256,256]{1,0:T(8,128)S(1)}, u32[]{:S(2)}, u32[]{:S(2)}) collective-permute-start(f32[256,256]{1,0:T(8,128)S(1)} %copy-done.1), channel_id=1, source_target_pairs={{0,6},{1,7},{2,0},{3,1},{4,2},{5,3},{6,4},{7,5},{8,14},{9,15},{10,... | collective-permute-start | bytes 786440 | tf_op jit(solution)/shard_map/ppermute | solution.py:35
  39.1 16.5 %collective-permute-start.6 = (f32[256,256]{1,0:T(8,128)S(1)}, f32[256,256]{1,0:T(8,128)S(1)}, u32[]{:S(2)}, u32[]{:S(2)}) collective-permute-start(f32[256,256]{1,0:T(8,128)S(1)} %copy-done.1), channel_id=1, source_target_pairs={{0,7},{1,0},{2,1},{3,2},{4,3},{5,4},{6,5},{7,6},{8,15},{9,8},{10,9... | collective-permute-start | bytes 786440 | tf_op jit(solution)/shard_map/ppermute | solution.py:35
  116.9 5.7 %collective-permute-start.14 = (f32[2,2048]{1,0:T(2,128)S(1)}, f32[2,2048]{1,0:T(2,128)S(1)}, u32[]{:S(2)}, u32[]{:S(2)}) collective-permute-start(f32[2,2048]{1,0:T(2,128)S(1)} %pad_maximum_fusion.10), channel_id=1, source_target_pairs={{0,2},{1,3},{2,4},{3,5},{4,6},{5,7},{6,0},{7,1},{8,10},{9,11},{10,... | collective-permute-start | bytes 49160 | tf_op jit(solution)/shard_map/ppermute | solution.py:50
  118.4 5.2 %collective-permute-start.15 = (f32[2,2048]{1,0:T(2,128)S(1)}, f32[2,2048]{1,0:T(2,128)S(1)}, u32[]{:S(2)}, u32[]{:S(2)}) collective-permute-start(f32[2,2048]{1,0:T(2,128)S(1)} %pad_maximum_fusion.10), channel_id=1, source_target_pairs={{0,4},{1,5},{2,6},{3,7},{4,0},{5,1},{6,2},{7,3},{8,12},{9,13},{10,... | collective-permute-start | bytes 49160 | tf_op jit(solution)/shard_map/ppermute | solution.py:50
  153.5 5.4 %collective-permute-start.18 = (f32[2,4096]{1,0:T(2,128)S(1)}, f32[2,4096]{1,0:T(2,128)S(1)}, u32[]{:S(2)}, u32[]{:S(2)}) collective-permute-start(f32[2,4096]{1,0:T(2,128)S(1)} %pad_maximum_fusion.3), channel_id=1, source_target_pairs={{0,16},{8,24},{16,0},{24,8},{32,48},{40,56},{48,32},{56,40},{64,80... | collective-permute-start | bytes 98312 | tf_op jit(solution)/shard_map/ppermute | solution.py:50
  160.3 5.2 %collective-permute-start.20 = (f32[2,4096]{1,0:T(2,128)S(1)}, f32[2,4096]{1,0:T(2,128)S(1)}, u32[]{:S(2)}, u32[]{:S(2)}) collective-permute-start(f32[2,4096]{1,0:T(2,128)S(1)} %pad_maximum_fusion.4), channel_id=1, source_target_pairs={{0,32},{8,40},{16,48},{24,56},{32,64},{40,72},{48,80},{56,88},{64,... | collective-permute-start | bytes 98312 | tf_op jit(solution)/shard_map/ppermute | solution.py:50
  160.5 5.4 %collective-permute-start.21 = (f32[2,4096]{1,0:T(2,128)S(1)}, f32[2,4096]{1,0:T(2,128)S(1)}, u32[]{:S(2)}, u32[]{:S(2)}) collective-permute-start(f32[2,4096]{1,0:T(2,128)S(1)} %pad_maximum_fusion.4), channel_id=1, source_target_pairs={{0,64},{8,72},{16,80},{24,88},{32,96},{40,104},{48,112},{56,120},{... | collective-permute-start | bytes 98312 | tf_op jit(solution)/shard_map/ppermute | solution.py:50
  180.0 5.7 %collective-permute-start.25 = (f32[2,2048]{1,0:T(2,128)S(1)}, f32[2,2048]{1,0:T(2,128)S(1)}, u32[]{:S(2)}, u32[]{:S(2)}) collective-permute-start(f32[2,2048]{1,0:T(2,128)S(1)} %pad_maximum_fusion.12), channel_id=1, source_target_pairs={{0,4},{1,5},{2,6},{3,7},{4,0},{5,1},{6,2},{7,3},{8,12},{9,13},{10,... | collective-permute-start | bytes 49160 | tf_op jit(solution)/shard_map/ppermute | solution.py:50
  201.5 5.4 %collective-permute-start.28 = (f32[2,4096]{1,0:T(2,128)S(1)}, f32[2,4096]{1,0:T(2,128)S(1)}, u32[]{:S(2)}, u32[]{:S(2)}) collective-permute-start(f32[2,4096]{1,0:T(2,128)S(1)} %pad_maximum_fusion.5), channel_id=1, source_target_pairs={{0,16},{8,24},{16,0},{24,8},{32,48},{40,56},{48,32},{56,40},{64,80... | collective-permute-start | bytes 98312 | tf_op jit(solution)/shard_map/ppermute | solution.py:50
  209.7 5.4 %collective-permute-start.31 = (f32[2,4096]{1,0:T(2,128)S(1)}, f32[2,4096]{1,0:T(2,128)S(1)}, u32[]{:S(2)}, u32[]{:S(2)}) collective-permute-start(f32[2,4096]{1,0:T(2,128)S(1)} %pad_maximum_fusion.6), channel_id=1, source_target_pairs={{0,64},{8,72},{16,80},{24,88},{32,96},{40,104},{48,112},{56,120},{... | collective-permute-start | bytes 98312 | tf_op jit(solution)/shard_map/ppermute | solution.py:50
  229.0 5.3 %collective-permute-start.35 = (f32[2,2048]{1,0:T(2,128)S(1)}, f32[2,2048]{1,0:T(2,128)S(1)}, u32[]{:S(2)}, u32[]{:S(2)}) collective-permute-start(f32[2,2048]{1,0:T(2,128)S(1)} %pad_maximum_fusion.14), channel_id=1, source_target_pairs={{0,4},{1,5},{2,6},{3,7},{4,0},{5,1},{6,2},{7,3},{8,12},{9,13},{10,... | collective-permute-start | bytes 49160 | tf_op jit(solution)/shard_map/ppermute | solution.py:50
  248.0 5.5 %collective-permute-start.38 = (f32[2,4096]{1,0:T(2,128)S(1)}, f32[2,4096]{1,0:T(2,128)S(1)}, u32[]{:S(2)}, u32[]{:S(2)}) collective-permute-start(f32[2,4096]{1,0:T(2,128)S(1)} %pad_maximum_fusion.7), channel_id=1, source_target_pairs={{0,16},{8,24},{16,0},{24,8},{32,48},{40,56},{48,32},{56,40},{64,80... | collective-permute-start | bytes 98312 | tf_op jit(solution)/shard_map/ppermute | solution.py:50
  254.9 5.5 %collective-permute-start.41 = (f32[2,4096]{1,0:T(2,128)S(1)}, f32[2,4096]{1,0:T(2,128)S(1)}, u32[]{:S(2)}, u32[]{:S(2)}) collective-permute-start(f32[2,4096]{1,0:T(2,128)S(1)} %pad_maximum_fusion.8), channel_id=1, source_target_pairs={{0,64},{8,72},{16,80},{24,88},{32,96},{40,104},{48,112},{56,120},{... | collective-permute-start | bytes 98312 | tf_op jit(solution)/shard_map/ppermute | solution.py:50
  (23 other events, 134.1 us)
Sparse Core Ops, SparseCore 0:
  10.1 53.0 all-gather.1
where the time goes:
time: 270 us; the launch traced here: 269 us
  other arithmetic  85.2 us (32%)
  starting transfers between devices  60.7 us (22%)
  waiting for transfers between devices  59.9 us (22%)
  matrix products  34.8 us (13%)
  between operations  15.3 us (6%)
  local copies, waits for them, and re-layouts  13.4 us (5%)
    ppermute x30, starting transfers between devices, combine_over(): lax.ppermute(packed, axis, digit_partners(axis, size, stride, width, k))  40.3 us
    dot_general x1, matrix products, inner_costs(): lax.dot_general(left, right, (((1,), (1,)), ((), ())), precision=lax.Prec...  34.8 us
    reduce_sum x3, other arithmetic, logsum_col(): totals = jnp.sum(jnp.exp(gaps / scale - peak[:, None]), axis=1)  30.6 us
    ppermute x30, waiting for transfers between devices, combine_over(): lax.ppermute(packed, axis, digit_partners(axis, size, stride, width, k))  29.3 us
    ppermute x13, waiting for transfers between devices, exchange(): lax.ppermute(x, axis, digit_partners(axis, size, stride, width, k))  23.6 us
    reduce_max x3, other arithmetic, logsum_row(): peak = jnp.max(gaps, axis=0) / scale  23.2 us
    reduce_sum x3, other arithmetic, logsum_row(): totals = jnp.sum(jnp.exp(gaps / scale - peak[None, :]), axis=0)  22.9 us
    ppermute x13, starting transfers between devices, exchange(): lax.ppermute(x, axis, digit_partners(axis, size, stride, width, k))  20.3 us
  transfers between devices with their start and end apart: 44, of which 37 were waited for; matrix products, arithmetic and copies ran while one was open for 1% of the time, Pallas kernels for 0%

commit v1 on v0

--- a/solution.py
+++ b/solution.py
@@ -5,6 +5,14 @@
 from jax.sharding import PartitionSpec as P
 
 ITERS = 3
+
+
+def gather_by_exchange(shard, axis, dim):
+    length = lax.axis_size(axis)
+    repeats = [length if d == dim else 1 for d in range(shard.ndim)]
+    return lax.all_to_all(
+        jnp.tile(shard, repeats), axis, split_axis=dim, concat_axis=dim, tiled=True
+    )
 
 
 def inner_costs(left, right):
@@ -113,8 +121,7 @@
     rows = passages.shape[0]
     split = rows - rows * 5 // 32
     passage_block = jnp.concatenate(
-        [lax.all_gather(passages[:split], "row", axis=0, tiled=True), gather_row(passages[split:])],
-        axis=0,
+        [gather_by_exchange(passages[:split], "row", 0), gather_row(passages[split:])], axis=0
     )
     cost_tile = inner_costs(query_block, passage_block)
     col_potential = jnp.zeros((cost_tile.shape[1],), jnp.float32)

time: 270 us -> 296 us (1.096)
  waiting for transfers between devices: 59.9 us -> 77.5 us
  starting transfers between devices: 60.7 us -> 74.9 us
  between operations: 15.3 us -> 2.27 us
  local copies, waits for them, and re-layouts: 13.4 us -> 18.3 us
    ppermute x13, waiting for transfers between devices: 23.6 us -> 49.1 us  [exchange(): lax.ppermute(x, axis, digit_partners(axis, size, stride, width, k))]
    ppermute x30, starting transfers between devices: 40.3 us -> 49.4 us  [combine_over(): lax.ppermute(packed, axis, digit_partners(axis, size, stride, width, k))]
    all_gather x1 -> x0, waiting for transfers between devices: 6.99 us -> none  [per_device(): lax.all_gather(passages[:split], 'row', axis=0, tiled=True)]
    all_to_all x0 -> x1, starting transfers between devices: none -> 5.53 us  [gather_by_exchange(): lax.all_to_all(jnp.tile(shard, repeats), axis, split_axis=dim, concat_axi...]
    unnamed x25 -> x29, local copies, waits for them, and re-layouts: 10.5 us -> 13.5 us
  transfers between devices with their start and end apart: 44 -> 44, of which waited for: 37 -> 34; matrix products, arithmetic and copies ran while one was open for 1% -> 3% of each run, Pallas kernels for 0% -> 0%
where the time goes in v1:
time: 296 us; the launch traced here: 295 us
  other arithmetic  87.3 us (29%)
  waiting for transfers between devices  77.5 us (26%)
  starting transfers between devices  74.9 us (25%)
  matrix products  34.8 us (12%)
  local copies, waits for them, and re-layouts  18.3 us (6%)
    ppermute x30, starting transfers between devices, combine_over(): lax.ppermute(packed, axis, digit_partners(axis, size, stride, width, k))  49.4 us
    ppermute x13, waiting for transfers between devices, exchange(): lax.ppermute(x, axis, digit_partners(axis, size, stride, width, k))  49.1 us
    dot_general x1, matrix products, inner_costs(): lax.dot_general(left, right, (((1,), (1,)), ((), ())), precision=lax.Prec...  34.8 us
    reduce_sum x3, other arithmetic, logsum_col(): totals = jnp.sum(jnp.exp(gaps / scale - peak[:, None]), axis=1)  31 us
    ppermute x30, waiting for transfers between devices, combine_over(): lax.ppermute(packed, axis, digit_partners(axis, size, stride, width, k))  28.3 us
    reduce_max x3, other arithmetic, logsum_row(): peak = jnp.max(gaps, axis=0) / scale  23.2 us
    reduce_sum x3, other arithmetic, logsum_row(): totals = jnp.sum(jnp.exp(gaps / scale - peak[None, :]), axis=0)  22.9 us
    ppermute x13, starting transfers between devices, exchange(): lax.ppermute(x, axis, digit_partners(axis, size, stride, width, k))  19.9 us
  transfers between devices with their start and end apart: 44, of which 34 were waited for; matrix products, arithmetic and copies ran while one was open for 3% of the time, Pallas kernels for 0%

profile of v1, /device:TPU:0, one launch (start us, length us, event | category | flops | bytes accessed | tf_op | source)
XLA Modules:
  0.0 295.0 jit_solution(11168883306346945445)
XLA Ops:
  3.7 2.9 collective-permute-start.8
  12.4 5.5 %all-to-all-start = ((f32[16,216,256]{2,1,0:T(8,128)}), f32[16,216,256]{2,1,0:T(8,128)S(1)}, u32[]{:S(2)}, u32[]{:S(2)}) async-start(f32[16,216,256]{2,1,0:T(8,128)} %tile.2), calls=%async_computation | async-start | bytes 7077888 | tf_op jit(solution)/shard_map/all_to_all | solution.py:13
  26.7 32.7 %collective-permute-done.10 = f32[160,256]{1,0:T(8,128)S(1)} collective-permute-done((f32[160,256]{1,0:T(8,128)S(1)}, f32[160,256]{1,0:T(8,128)S(1)}, u32[]{:S(2)}, u32[]{:S(2)}) %collective-permute-start.10) | collective-permute-done | bytes 163872 | tf_op jit(solution)/shard_map/ppermute | solution.py:43
  60.3 3.0 %collective-permute-done.11 = f32[160,256]{1,0:T(8,128)S(1)} collective-permute-done((f32[160,256]{1,0:T(8,128)S(1)}, f32[160,256]{1,0:T(8,128)S(1)}, u32[]{:S(2)}, u32[]{:S(2)}) %collective-permute-start.11) | collective-permute-done | bytes 163872 | tf_op jit(solution)/shard_map/ppermute | solution.py:43
  68.1 2.9 collective-permute-start.5
  77.2 6.5 %collective-permute-done.5 = f32[256,256]{1,0:T(8,128)S(1)} collective-permute-done((f32[256,256]{1,0:T(8,128)}, f32[256,256]{1,0:T(8,128)S(1)}, u32[]{:S(2)}, u32[]{:S(2)}) %collective-permute-start.5) | collective-permute-done | bytes 262176 | tf_op jit(solution)/shard_map/ppermute | solution.py:43
  90.2 34.8 %subtract_reduce_fusion.5 = (f32[2048]{0:T(1024)S(1)}, f32[2048,4096]{1,0:T(8,128)}) fusion(f32[2048,256]{1,0:T(8,128)S(1)} %copy-done.2, f32[4096,256]{1,0:T(8,128)S(1)} %bitcast_dynamic-update-slice_fusion.16, f32[4096]{0:T(1024)S(1)} %multiply_reduce_fusion, f32[2048]{0:T(1024)S(1)} %multiply_reduce_fusion.1), kind=kOutput, calls=%fused_computation.12 | convolution fusion | flops 25811744768 | bytes 39878656 | tf_op jit(solution)/shard_map/dot_general | solution.py:21
  125.0 14.5 %exponential_reduce_fusion.5 = f32[2048]{0:T(1024)S(1)} fusion(f32[2048,4096]{1,0:T(8,128)} %get-tuple-element.59, f32[2048]{0:T(1024)S(1)} %broadcast_divide_fusion.5, f32[]{:T(128)} %bitcast), kind=kLoop, calls=%fused_computation.5 | loop fusion | flops 33552384 | bytes 33570820 | tf_op jit(solution)/shard_map/reduce_sum | solution.py:91
  149.3 13.8 %subtract_reduce_fusion.4 = f32[4096]{0:T(1024)S(1)} fusion(f32[2048,4096]{1,0:T(8,128)} %get-tuple-element.59, f32[2048]{0:T(1024)S(1)} %multiply_subtract_fusion.6), kind=kLoop, calls=%fused_computation.11 | loop fusion | flops 16773120 | bytes 33579008 | tf_op jit(solution)/shard_map/reduce_max | solution.py:96
  163.1 6.3 %copy-done = f32[2048,4096]{1,0:T(8,128)S(1)} copy-done((f32[2048,4096]{1,0:T(8,128)S(1)}, f32[2048,4096]{1,0:T(8,128)}, u32[]{:S(2)}) %copy-start) | copy-done | bytes 33554456
  169.5 7.6 %exponential_reduce_fusion.4 = f32[4096]{0:T(1024)S(1)} fusion(f32[2048,4096]{1,0:T(8,128)S(1)} %copy-done, f32[4096]{0:T(1024)S(1)} %broadcast_divide_fusion.2, f32[2048]{0:T(1024)S(1)} %multiply_subtract_fusion.6, f32[]{:T(128)} %bitcast), kind=kLoop, calls=%fused_computation.4 | loop fusion | flops 33550336 | bytes 33595396 | tf_op jit(solution)/shard_map/reduce_sum | solution.py:97
  177.1 3.4 %collective-permute-start.17 = (f32[2,4096]{1,0:T(2,128)S(1)}, f32[2,4096]{1,0:T(2,128)S(1)}, u32[]{:S(2)}, u32[]{:S(2)}) collective-permute-start(f32[2,4096]{1,0:T(2,128)S(1)} %pad_maximum_fusion.3), channel_id=1, source_target_pairs={{0,8},{8,16},{16,24},{24,0},{32,40},{40,48},{48,56},{56,32},{64,72... | collective-permute-start | bytes 98312 | tf_op jit(solution)/shard_map/ppermute | solution.py:58
  180.5 5.7 %collective-permute-start.18 = (f32[2,4096]{1,0:T(2,128)S(1)}, f32[2,4096]{1,0:T(2,128)S(1)}, u32[]{:S(2)}, u32[]{:S(2)}) collective-permute-start(f32[2,4096]{1,0:T(2,128)S(1)} %pad_maximum_fusion.3), channel_id=1, source_target_pairs={{0,16},{8,24},{16,0},{24,8},{32,48},{40,56},{48,32},{56,40},{64,80... | collective-permute-start | bytes 98312 | tf_op jit(solution)/shard_map/ppermute | solution.py:58
  197.5 3.0 %subtract_reduce_fusion.3 = f32[2048]{0:T(1024)S(1)} fusion(f32[2048,4096]{1,0:T(8,128)S(1)} %copy-done, f32[4096]{0:T(1024)S(1)} %bitcast.128), kind=kLoop, calls=%fused_computation.10 | loop fusion | flops 16775168 | bytes 33579008 | tf_op jit(solution)/shard_map/reduce_max | solution.py:90
  200.5 8.2 %exponential_reduce_fusion.3 = f32[2048]{0:T(1024)S(1)} fusion(f32[2048,4096]{1,0:T(8,128)S(1)} %copy-done, f32[2048]{0:T(1024)S(1)} %broadcast_divide_fusion.4, f32[4096]{0:T(1024)S(1)} %bitcast.129, f32[]{:T(128)} %bitcast), kind=kLoop, calls=%fused_computation.3 | loop fusion | flops 33552384 | bytes 33587204 | tf_op jit(solution)/shard_map/reduce_sum | solution.py:91
  210.4 3.8 %collective-permute-start.25 = (f32[2,2048]{1,0:T(2,128)S(1)}, f32[2,2048]{1,0:T(2,128)S(1)}, u32[]{:S(2)}, u32[]{:S(2)}) collective-permute-start(f32[2,2048]{1,0:T(2,128)S(1)} %pad_maximum_fusion.12), channel_id=1, source_target_pairs={{0,4},{1,5},{2,6},{3,7},{4,0},{5,1},{6,2},{7,3},{8,12},{9,13},{10,... | collective-permute-start | bytes 49160 | tf_op jit(solution)/shard_map/ppermute | solution.py:58
  218.0 4.7 %subtract_reduce_fusion.2 = f32[4096]{0:T(1024)S(1)} fusion(f32[2048,4096]{1,0:T(8,128)S(1)} %copy-done, f32[2048]{0:T(1024)S(1)} %multiply_subtract_fusion.5), kind=kLoop, calls=%fused_computation.9 | loop fusion | flops 16773120 | bytes 33579008 | tf_op jit(solution)/shard_map/reduce_max | solution.py:96
  222.7 7.6 %exponential_reduce_fusion.2 = f32[4096]{0:T(1024)S(1)} fusion(f32[2048,4096]{1,0:T(8,128)S(1)} %copy-done, f32[4096]{0:T(1024)S(1)} %broadcast_divide_fusion.1, f32[2048]{0:T(1024)S(1)} %multiply_subtract_fusion.5, f32[]{:T(128)} %bitcast), kind=kLoop, calls=%fused_computation.2 | loop fusion | flops 33550336 | bytes 33595396 | tf_op jit(solution)/shard_map/reduce_sum | solution.py:97
  231.6 3.8 %collective-permute-start.28 = (f32[2,4096]{1,0:T(2,128)S(1)}, f32[2,4096]{1,0:T(2,128)S(1)}, u32[]{:S(2)}, u32[]{:S(2)}) collective-permute-start(f32[2,4096]{1,0:T(2,128)S(1)} %pad_maximum_fusion.5), channel_id=1, source_target_pairs={{0,16},{8,24},{16,0},{24,8},{32,48},{40,56},{48,32},{56,40},{64,80... | collective-permute-start | bytes 98312 | tf_op jit(solution)/shard_map/ppermute | solution.py:58
  240.8 3.8 %collective-permute-start.31 = (f32[2,4096]{1,0:T(2,128)S(1)}, f32[2,4096]{1,0:T(2,128)S(1)}, u32[]{:S(2)}, u32[]{:S(2)}) collective-permute-start(f32[2,4096]{1,0:T(2,128)S(1)} %pad_maximum_fusion.6), channel_id=1, source_target_pairs={{0,64},{8,72},{16,80},{24,88},{32,96},{40,104},{48,112},{56,120},{... | collective-permute-start | bytes 98312 | tf_op jit(solution)/shard_map/ppermute | solution.py:58
  248.7 3.0 %subtract_reduce_fusion.1 = f32[2048]{0:T(1024)S(1)} fusion(f32[2048,4096]{1,0:T(8,128)S(1)} %copy-done, f32[4096]{0:T(1024)S(1)} %bitcast.130), kind=kLoop, calls=%fused_computation.8 | loop fusion | flops 16775168 | bytes 33579008 | tf_op jit(solution)/shard_map/reduce_max | solution.py:90
  251.7 8.2 %exponential_reduce_fusion.1 = f32[2048]{0:T(1024)S(1)} fusion(f32[2048,4096]{1,0:T(8,128)S(1)} %copy-done, f32[2048]{0:T(1024)S(1)} %broadcast_divide_fusion.3, f32[4096]{0:T(1024)S(1)} %bitcast.131, f32[]{:T(128)} %bitcast), kind=kLoop, calls=%fused_computation.1 | loop fusion | flops 33552384 | bytes 33587204 | tf_op jit(solution)/shard_map/reduce_sum | solution.py:91
  268.0 4.7 %subtract_reduce_fusion = f32[4096]{0:T(1024)S(1)} fusion(f32[2048,4096]{1,0:T(8,128)S(1)} %copy-done, f32[2048]{0:T(1024)S(1)} %multiply_subtract_fusion.4), kind=kLoop, calls=%fused_computation.7 | loop fusion | flops 16773120 | bytes 33579008 | tf_op jit(solution)/shard_map/reduce_max | solution.py:96
  272.8 7.6 %exponential_reduce_fusion = f32[4096]{0:T(1024)S(1)} fusion(f32[2048,4096]{1,0:T(8,128)S(1)} %copy-done, f32[4096]{0:T(1024)S(1)} %broadcast_divide_fusion, f32[2048]{0:T(1024)S(1)} %multiply_subtract_fusion.4, f32[]{:T(128)} %bitcast), kind=kLoop, calls=%fused_computation | loop fusion | flops 33550336 | bytes 33595396 | tf_op jit(solution)/shard_map/reduce_sum | solution.py:97
  (163 shorter events, 94.5 us)
Async XLA Ops:
  2.0 16.9 %collective-permute-start.7 = (f32[40,256]{1,0:T(8,128)}, f32[40,256]{1,0:T(8,128)}, u32[]{:S(2)}, u32[]{:S(2)}) collective-permute-start(f32[40,256]{1,0:T(8,128)} %get-tuple-element.7), channel_id=1, source_target_pairs={{0,8},{8,16},{16,24},{24,0},{32,40},{40,48},{48,56},{56,32},{64,72... | collective-permute-start | bytes 122888 | tf_op jit(solution)/shard_map/ppermute | solution.py:43
  3.7 15.3 %collective-permute-start.8 = (f32[40,256]{1,0:T(8,128)}, f32[40,256]{1,0:T(8,128)}, u32[]{:S(2)}, u32[]{:S(2)}) collective-permute-start(f32[40,256]{1,0:T(8,128)} %get-tuple-element.7), channel_id=1, source_target_pairs={{0,16},{8,24},{16,0},{24,8},{32,48},{40,56},{48,32},{56,40},{64,80... | collective-permute-start | bytes 122888 | tf_op jit(solution)/shard_map/ppermute | solution.py:43
  6.6 12.4 %collective-permute-start.9 = (f32[40,256]{1,0:T(8,128)}, f32[40,256]{1,0:T(8,128)}, u32[]{:S(2)}, u32[]{:S(2)}) collective-permute-start(f32[40,256]{1,0:T(8,128)} %get-tuple-element.7), channel_id=1, source_target_pairs={{0,24},{8,0},{16,8},{24,16},{32,56},{40,32},{48,40},{56,48},{64,88... | collective-permute-start | bytes 122888 | tf_op jit(solution)/shard_map/ppermute | solution.py:43
  8.0 60.1 %collective-permute-start = (f32[256,256]{1,0:T(8,128)}, f32[256,256]{1,0:T(8,128)}, u32[]{:S(2)}, u32[]{:S(2)}) collective-permute-start(f32[256,256]{1,0:T(8,128)} %param.3), channel_id=1, source_target_pairs={{0,1},{1,2},{2,3},{3,4},{4,5},{5,6},{6,7},{7,0},{8,9},{9,10},{10,1... | collective-permute-start | bytes 786440 | tf_op jit(solution)/shard_map/ppermute | solution.py:43
  8.0 64.0 %collective-permute-start.1 = (f32[256,256]{1,0:T(8,128)}, f32[256,256]{1,0:T(8,128)}, u32[]{:S(2)}, u32[]{:S(2)}) collective-permute-start(f32[256,256]{1,0:T(8,128)} %param.3), channel_id=1, source_target_pairs={{0,2},{1,3},{2,4},{3,5},{4,6},{5,7},{6,0},{7,1},{8,10},{9,11},{10,... | collective-permute-start | bytes 786440 | tf_op jit(solution)/shard_map/ppermute | solution.py:43
  12.4 75.1 %all-to-all-start = ((f32[16,216,256]{2,1,0:T(8,128)}), f32[16,216,256]{2,1,0:T(8,128)S(1)}, u32[]{:S(2)}, u32[]{:S(2)}) async-start(f32[16,216,256]{2,1,0:T(8,128)} %tile.2), calls=%async_computation | async-start | bytes 7077888 | tf_op jit(solution)/shard_map/all_to_all | solution.py:13
  19.9 39.5 %collective-permute-start.10 = (f32[160,256]{1,0:T(8,128)S(1)}, f32[160,256]{1,0:T(8,128)S(1)}, u32[]{:S(2)}, u32[]{:S(2)}) collective-permute-start(f32[160,256]{1,0:T(8,128)S(1)} %get-tuple-element.9), channel_id=1, source_target_pairs={{0,32},{8,40},{16,48},{24,56},{32,64},{40,72},{48,80},{56,88},{64,... | collective-permute-start | bytes 491528 | tf_op jit(solution)/shard_map/ppermute | solution.py:43
  21.6 41.6 %collective-permute-start.11 = (f32[160,256]{1,0:T(8,128)S(1)}, f32[160,256]{1,0:T(8,128)S(1)}, u32[]{:S(2)}, u32[]{:S(2)}) collective-permute-start(f32[160,256]{1,0:T(8,128)S(1)} %get-tuple-element.9), channel_id=1, source_target_pairs={{0,64},{8,72},{16,80},{24,88},{32,96},{40,104},{48,112},{56,120},{... | collective-permute-start | bytes 491528 | tf_op jit(solution)/shard_map/ppermute | solution.py:43
  24.3 42.3 %collective-permute-start.12 = (f32[160,256]{1,0:T(8,128)S(1)}, f32[160,256]{1,0:T(8,128)S(1)}, u32[]{:S(2)}, u32[]{:S(2)}) collective-permute-start(f32[160,256]{1,0:T(8,128)S(1)} %get-tuple-element.9), channel_id=1, source_target_pairs={{0,96},{8,104},{16,112},{24,120},{32,0},{40,8},{48,16},{56,24},{64... | collective-permute-start | bytes 491528 | tf_op jit(solution)/shard_map/ppermute | solution.py:43
  59.5 13.5 %collective-permute-start.2 = (f32[256,256]{1,0:T(8,128)}, f32[256,256]{1,0:T(8,128)S(1)}, u32[]{:S(2)}, u32[]{:S(2)}) collective-permute-start(f32[256,256]{1,0:T(8,128)} %param.3), channel_id=1, source_target_pairs={{0,3},{1,4},{2,5},{3,6},{4,7},{5,0},{6,1},{7,2},{8,11},{9,12},{10,... | collective-permute-start | bytes 786440 | tf_op jit(solution)/shard_map/ppermute | solution.py:43
  63.3 12.1 %collective-permute-start.3 = (f32[256,256]{1,0:T(8,128)}, f32[256,256]{1,0:T(8,128)S(1)}, u32[]{:S(2)}, u32[]{:S(2)}) collective-permute-start(f32[256,256]{1,0:T(8,128)} %param.3), channel_id=1, source_target_pairs={{0,4},{1,5},{2,6},{3,7},{4,0},{5,1},{6,2},{7,3},{8,12},{9,13},{10,... | collective-permute-start | bytes 786440 | tf_op jit(solution)/shard_map/ppermute | solution.py:43
  66.6 10.5 %collective-permute-start.4 = (f32[256,256]{1,0:T(8,128)}, f32[256,256]{1,0:T(8,128)S(1)}, u32[]{:S(2)}, u32[]{:S(2)}) collective-permute-start(f32[256,256]{1,0:T(8,128)} %param.3), channel_id=1, source_target_pairs={{0,5},{1,6},{2,7},{3,0},{4,1},{5,2},{6,3},{7,4},{8,13},{9,14},{10,... | collective-permute-start | bytes 786440 | tf_op jit(solution)/shard_map/ppermute | solution.py:43
  68.1 15.5 %collective-permute-start.5 = (f32[256,256]{1,0:T(8,128)}, f32[256,256]{1,0:T(8,128)S(1)}, u32[]{:S(2)}, u32[]{:S(2)}) collective-permute-start(f32[256,256]{1,0:T(8,128)} %param.3), channel_id=1, source_target_pairs={{0,6},{1,7},{2,0},{3,1},{4,2},{5,3},{6,4},{7,5},{8,14},{9,15},{10,... | collective-permute-start | bytes 786440 | tf_op jit(solution)/shard_map/ppermute | solution.py:43
  72.0 13.5 %collective-permute-start.6 = (f32[256,256]{1,0:T(8,128)}, f32[256,256]{1,0:T(8,128)S(1)}, u32[]{:S(2)}, u32[]{:S(2)}) collective-permute-start(f32[256,256]{1,0:T(8,128)} %param.3), channel_id=1, source_target_pairs={{0,7},{1,0},{2,1},{3,2},{4,3},{5,4},{6,5},{7,6},{8,15},{9,8},{10,9... | collective-permute-start | bytes 786440 | tf_op jit(solution)/shard_map/ppermute | solution.py:43
  177.1 10.5 %collective-permute-start.17 = (f32[2,4096]{1,0:T(2,128)S(1)}, f32[2,4096]{1,0:T(2,128)S(1)}, u32[]{:S(2)}, u32[]{:S(2)}) collective-permute-start(f32[2,4096]{1,0:T(2,128)S(1)} %pad_maximum_fusion.3), channel_id=1, source_target_pairs={{0,8},{8,16},{16,24},{24,0},{32,40},{40,48},{48,56},{56,32},{64,72... | collective-permute-start | bytes 98312 | tf_op jit(solution)/shard_map/ppermute | solution.py:58
  180.5 7.9 %collective-permute-start.18 = (f32[2,4096]{1,0:T(2,128)S(1)}, f32[2,4096]{1,0:T(2,128)S(1)}, u32[]{:S(2)}, u32[]{:S(2)}) collective-permute-start(f32[2,4096]{1,0:T(2,128)S(1)} %pad_maximum_fusion.3), channel_id=1, source_target_pairs={{0,16},{8,24},{16,0},{24,8},{32,48},{40,56},{48,32},{56,40},{64,80... | collective-permute-start | bytes 98312 | tf_op jit(solution)/shard_map/ppermute | solution.py:58
  190.3 5.4 %collective-permute-start.20 = (f32[2,4096]{1,0:T(2,128)S(1)}, f32[2,4096]{1,0:T(2,128)S(1)}, u32[]{:S(2)}, u32[]{:S(2)}) collective-permute-start(f32[2,4096]{1,0:T(2,128)S(1)} %pad_maximum_fusion.4), channel_id=1, source_target_pairs={{0,32},{8,40},{16,48},{24,56},{32,64},{40,72},{48,80},{56,88},{64,... | collective-permute-start | bytes 98312 | tf_op jit(solution)/shard_map/ppermute | solution.py:58
  210.4 5.7 %collective-permute-start.25 = (f32[2,2048]{1,0:T(2,128)S(1)}, f32[2,2048]{1,0:T(2,128)S(1)}, u32[]{:S(2)}, u32[]{:S(2)}) collective-permute-start(f32[2,2048]{1,0:T(2,128)S(1)} %pad_maximum_fusion.12), channel_id=1, source_target_pairs={{0,4},{1,5},{2,6},{3,7},{4,0},{5,1},{6,2},{7,3},{8,12},{9,13},{10,... | collective-permute-start | bytes 49160 | tf_op jit(solution)/shard_map/ppermute | solution.py:58
  230.4 5.5 %collective-permute-start.27 = (f32[2,4096]{1,0:T(2,128)S(1)}, f32[2,4096]{1,0:T(2,128)S(1)}, u32[]{:S(2)}, u32[]{:S(2)}) collective-permute-start(f32[2,4096]{1,0:T(2,128)S(1)} %pad_maximum_fusion.5), channel_id=1, source_target_pairs={{0,8},{8,16},{16,24},{24,0},{32,40},{40,48},{48,56},{56,32},{64,72... | collective-permute-start | bytes 98312 | tf_op jit(solution)/shard_map/ppermute | solution.py:58
  231.6 6.1 %collective-permute-start.28 = (f32[2,4096]{1,0:T(2,128)S(1)}, f32[2,4096]{1,0:T(2,128)S(1)}, u32[]{:S(2)}, u32[]{:S(2)}) collective-permute-start(f32[2,4096]{1,0:T(2,128)S(1)} %pad_maximum_fusion.5), channel_id=1, source_target_pairs={{0,16},{8,24},{16,0},{24,8},{32,48},{40,56},{48,32},{56,40},{64,80... | collective-permute-start | bytes 98312 | tf_op jit(solution)/shard_map/ppermute | solution.py:58
  239.5 5.5 %collective-permute-start.30 = (f32[2,4096]{1,0:T(2,128)S(1)}, f32[2,4096]{1,0:T(2,128)S(1)}, u32[]{:S(2)}, u32[]{:S(2)}) collective-permute-start(f32[2,4096]{1,0:T(2,128)S(1)} %pad_maximum_fusion.6), channel_id=1, source_target_pairs={{0,32},{8,40},{16,48},{24,56},{32,64},{40,72},{48,80},{56,88},{64,... | collective-permute-start | bytes 98312 | tf_op jit(solution)/shard_map/ppermute | solution.py:58
  240.8 6.1 %collective-permute-start.31 = (f32[2,4096]{1,0:T(2,128)S(1)}, f32[2,4096]{1,0:T(2,128)S(1)}, u32[]{:S(2)}, u32[]{:S(2)}) collective-permute-start(f32[2,4096]{1,0:T(2,128)S(1)} %pad_maximum_fusion.6), channel_id=1, source_target_pairs={{0,64},{8,72},{16,80},{24,88},{32,96},{40,104},{48,112},{56,120},{... | collective-permute-start | bytes 98312 | tf_op jit(solution)/shard_map/ppermute | solution.py:58
  280.6 5.5 %collective-permute-start.38 = (f32[2,4096]{1,0:T(2,128)S(1)}, f32[2,4096]{1,0:T(2,128)S(1)}, u32[]{:S(2)}, u32[]{:S(2)}) collective-permute-start(f32[2,4096]{1,0:T(2,128)S(1)} %pad_maximum_fusion.7), channel_id=1, source_target_pairs={{0,16},{8,24},{16,0},{24,8},{32,48},{40,56},{48,32},{56,40},{64,80... | collective-permute-start | bytes 98312 | tf_op jit(solution)/shard_map/ppermute | solution.py:58
  287.4 5.5 %collective-permute-start.41 = (f32[2,4096]{1,0:T(2,128)S(1)}, f32[2,4096]{1,0:T(2,128)S(1)}, u32[]{:S(2)}, u32[]{:S(2)}) collective-permute-start(f32[2,4096]{1,0:T(2,128)S(1)} %pad_maximum_fusion.8), channel_id=1, source_target_pairs={{0,64},{8,72},{16,80},{24,88},{32,96},{40,104},{48,112},{56,120},{... | collective-permute-start | bytes 98312 | tf_op jit(solution)/shard_map/ppermute | solution.py:58
  (25 other events, 109.8 us)
